TPU v7x, 256 devices: a whole 4x4x8 slice. The times are simulated.
256 devices in a mesh: ctx: 32 (over z, y_hi, core), mp: 8 (over x, y_lo).
Axes of the slice: x: 4, y: 4 (y_hi: 2, y_lo: 2; y = y_hi * 2 + y_lo), z: 8, core: 2. Of those that a mesh axis runs over, the one named last changes fastest.
Arguments:
- proj: bfloat16 [8192, 3, 8192], P(('ctx', 'mp')), may hold values from -6 to 6
- conv_weight: float32 [3, 7, 8192], replicated, may hold values from -2 to 2
- residues: float32 [128, 16], P('mp'), may hold values from -1.5 to 1.5
- decays: float32 [128, 16], P('mp'), may hold values from 1.2207031e-05 to 0.03
- doc_lengths: int32 [64], replicated, may hold values from 1 to 768, 8192 in all
Outputs:
- mixed: bfloat16 [8192, 8192], P(('ctx', 'mp'))
All inputs are finite; a program needn't handle non-finite values.
Results may differ from a plain program's by a relative error of at most 0.014.
Values may be sent and summed in bfloat16 or wider, within the bound.
No kernel may reach another device: no remote copies, remote signals or barrier semaphores. Data moves between devices by JAX's collectives and lax.ppermute only.
A program may use at most 64 MiB of HBM per device.

v0:
```python
import jax
import jax.numpy as jnp
from jax import lax
from jax.sharding import PartitionSpec as P


def shifted_2(block, axis, distance):
    devices = range(lax.axis_size(axis))
    route = [(i - distance, i) for i in devices if i - distance in devices]
    return lax.ppermute(block, axis, route)


def document_number_index(doc_lengths, positions):
    doc_starts = jnp.cumsum(doc_lengths) - doc_lengths
    inside = (doc_starts[None, :] <= positions[:, None]).astype(jnp.int32)
    return jnp.sum(inside, axis=1) - 1


def short_convolution(padded, conv_weight, padded_document_ids, padded_pos, out_rows):
    kernel_len = conv_weight.shape[1]
    result = jnp.zeros((out_rows,) + padded.shape[1:], jnp.float32)
    own_docs = padded_document_ids[kernel_len - 1 :]
    for position_shift in range(kernel_len):
        begin_row = kernel_len - 1 - position_shift
        earlier = padded[begin_row : begin_row + out_rows].astype(jnp.float32)
        keep_mask = (padded_document_ids[begin_row : begin_row + out_rows] == own_docs) & (
            padded_pos[begin_row : begin_row + out_rows] >= 0
        )
        result = (
            result
            + conv_weight[:, position_shift, :][None]
            * earlier
            * keep_mask.astype(jnp.float32)[:, None, None]
        )
    return result


def filter_tile(coefficient, decays, out_index, piece_start, width_in):
    span = float(width_in)
    out_float = (out_index - piece_start).astype(jnp.float32)
    shifted = jnp.maximum(out_float - span, -span)
    left_neighbor = coefficient[:, :, None] * jnp.exp(-decays[:, :, None] * shifted[None, None, :])
    in_offsets = jnp.arange(width_in).astype(jnp.float32)
    right_neighbor = jnp.exp(-decays[:, :, None] * (span - in_offsets)[None, None, :])
    token_tile_rows = jnp.einsum(
        "ejz,ejx->ezx", left_neighbor, right_neighbor, precision=lax.Precision.HIGHEST
    )
    lag_matrix = (out_index - piece_start)[:, None] - jnp.arange(width_in, dtype=jnp.int32)[None, :]
    return jnp.where((lag_matrix >= 0)[None], token_tile_rows, 0.0)


def split_product(form, weights, inputs):
    upper_part = weights.astype(jnp.bfloat16)
    lower_part = (weights - upper_part.astype(jnp.float32)).astype(jnp.bfloat16)
    first = jnp.einsum(form, upper_part, inputs, preferred_element_type=jnp.float32)
    return first + jnp.einsum(form, lower_part, inputs, preferred_element_type=jnp.float32)


def long_filter(product, residues, decays, block_begin_position):
    block_len = product.shape[0]
    channels = product.shape[1]
    group_count = residues.shape[0]
    group_width = channels // group_count
    coefficient = residues * jnp.sqrt(decays)
    out_index = block_begin_position + jnp.arange(block_len, dtype=jnp.int32)

    def one_tile(running, rows_part, part_start):
        width_in = rows_part.shape[0]
        token_tile_rows = filter_tile(coefficient, decays, out_index, part_start, width_in)
        inputs = rows_part.reshape(width_in, group_count, group_width)
        return running + split_product("grs,sgc->rgc", token_tile_rows, inputs)

    initial = jnp.zeros((block_len, group_count, group_width), jnp.float32)
    piece_rows = lax.all_gather(product, "ctx", axis=0, tiled=True)
    width_in = piece_rows.shape[0]
    count_blocks = width_in // block_len
    stacked = piece_rows.reshape(count_blocks, block_len, channels)
    starts = block_len * jnp.arange(count_blocks, dtype=jnp.int32)

    def scan_step(carry, pair):
        return (one_tile(carry, pair[0], pair[1]), None)

    result, unused = lax.scan(scan_step, initial, (stacked, starts))
    return result.reshape(block_len, channels).astype(jnp.bfloat16)


def shards(proj, conv_weight, residues, decays, doc_lengths):
    kernel_len = conv_weight.shape[1]
    channel_rows = lax.all_to_all(proj, "mp", split_axis=2, concat_axis=0, tiled=True)
    block_len = channel_rows.shape[0]
    channels = channel_rows.shape[2]
    local_weight = lax.dynamic_slice_in_dim(
        conv_weight, lax.axis_index("mp") * channels, channels, 2
    )
    tail_rows = shifted_2(channel_rows[block_len - (kernel_len - 1) :], "ctx", 1)
    block_begin_position = lax.axis_index("ctx") * block_len
    padded_pos = (
        block_begin_position
        - (kernel_len - 1)
        + jnp.arange(block_len + kernel_len - 1, dtype=jnp.int32)
    )
    padded_document_ids = document_number_index(doc_lengths, padded_pos)
    padded = jnp.concatenate([tail_rows, channel_rows], axis=0)
    conv = short_convolution(padded, local_weight, padded_document_ids, padded_pos, block_len)
    query_part = conv[:, 0]
    product = (conv[:, 1] * conv[:, 2]).astype(jnp.bfloat16)
    filtered = long_filter(product, residues, decays, block_begin_position)
    mixed_out = (query_part * filtered.astype(jnp.float32)).astype(jnp.bfloat16)
    return lax.all_to_all(mixed_out, "mp", split_axis=0, concat_axis=1, tiled=True)


def solution(mesh):
    return jax.shard_map(
        shards,
        mesh=mesh,
        in_specs=(P(("ctx", "mp"), None, None), P(), P("mp", None), P("mp", None), P()),
        out_specs=P(("ctx", "mp"), None),
        check_vma=False,
    )
```

profile of v0, /device:TPU:8, one launch (start us, length us, event | category | flops | bytes accessed | tf_op | source)
XLA Modules:
  0.0 531.1 jit_solution(9122464082286298592)
XLA Ops:
  6.5 10.6 %copy.23 = bf16[32,3,8192]{0,1,2:T(4,128)(2,1)} copy(bf16[32,3,8192]{2,0,1:T(8,128)(2,1)} %param.7) | data formatting | bytes 3145728 | tf_op args[0]
  17.2 9.8 %reshape.117 = bf16[8,2,49152]{2,1,0:T(2,128)(2,1)} reshape(bf16[8192,3,32]{2,1,0:T(4,128)(2,1)} %bitcast.54) | data formatting | bytes 3145728
  27.0 5.9 %all-to-all-start = ((bf16[8,2,49152]{2,1,0:T(2,128)(2,1)}), bf16[8,2,49152]{2,1,0:T(2,128)(2,1)S(1)}, u32[]{:S(2)}, u32[]{:S(2)}) async-start(bf16[8,2,49152]{2,1,0:T(2,128)(2,1)} %reshape.117), calls=%async_computation | async-start | bytes 3145728 | tf_op jit(solution)/shard_map/all_to_all | solution.py:89
  35.0 19.6 %all-to-all-done = bf16[8,2,49152]{2,1,0:T(2,128)(2,1)S(1)} async-done(((bf16[8,2,49152]{2,1,0:T(2,128)(2,1)}), bf16[8,2,49152]{2,1,0:T(2,128)(2,1)S(1)}, u32[]{:S(2)}, u32[]{:S(2)}) %all-to-all-start) | async-done | bytes 1572896 | tf_op jit(solution)/shard_map/all_to_all | solution.py:89
  54.7 7.6 %reshape.118 = bf16[8192,3,32]{2,1,0:T(4,128)(2,1)} reshape(bf16[8,2,49152]{2,1,0:T(2,128)(2,1)S(1)} %all-to-all-done) | data formatting | bytes 3145728
  62.3 10.5 %copy.31 = bf16[32,3,8,1024]{3,0,2,1:T(8,128)(2,1)S(1)} copy(bf16[32,3,8,1024]{0,1,3,2:T(4,128)(2,1)} %bitcast.53) | data formatting | bytes 3145728 | tf_op jit(solution)/shard_map/all_to_all | solution.py:89
  75.0 3.9 multiply_add_fusion
  80.4 142.8 %all-gather.3.cloned.1.call-done = bf16[8192,1,1024]{2,0,1:T(8,128)(2,1)} async-done(((bf16[256,1,1024]{2,0,1:T(8,128)(2,1)}), bf16[8192,1,1024]{2,0,1:T(8,128)(2,1)}) %all-gather.3.cloned.1.call-update) | async-done | bytes 16777232 | tf_op jit(solution)/shard_map/all_gather | solution.py:74
  223.1 282.1 %while.13 = (s32[]{:T(128)}, f32[256,16,64]{0,2,1:T(8,128)S(1)}, bf16[32,256,1024]{2,1,0:T(8,128)(2,1)}, s32[32]{0:T(128)S(1)}, f32[16,16]{1,0:T(8,128)S(1)}, /*...) while((s32[]{:T(128)}, f32[256,16,64]{0,2,1:T(8,128)S(1)}, ...), condition=%wide.region_3.4_spmd.clone, body=%wide.region_2.3_spmd.clone.sunk | while | flops 477169920 | bytes 20127888 | solution.py:83
  226.4 3.7 fusion.42
  235.3 3.7 fusion.42
  244.1 3.7 fusion.42
  252.9 3.7 fusion.42
  270.5 3.7 fusion.42
  279.3 3.7 fusion.42
  288.2 3.7 fusion.42
  297.0 3.7 fusion.42
  305.8 3.7 fusion.42
  314.6 3.7 fusion.42
  358.7 3.7 fusion.42
  367.5 3.7 fusion.42
  376.3 3.7 fusion.42
  385.1 3.7 fusion.42
  394.0 3.7 fusion.42
  402.8 3.7 fusion.42
  438.1 3.7 fusion.42
  446.9 3.7 fusion.42
  455.7 3.7 fusion.42
  464.5 3.7 fusion.42
  473.3 3.7 fusion.42
  482.1 3.7 fusion.42
  508.6 14.8 %all_to_all.34 = bf16[8,32,1024]{2,1,0:T(8,128)(2,1)S(1)} all-to-all(bf16[8,32,1024]{2,1,0:T(8,128)(2,1)S(1)} %multiply_convert_fusion), channel_id=1, replica_groups=mesh['ctx'=32,'mp'=8] {'mp'}, dimensions={0} | all-to-all | bytes 1048576 | tf_op jit(solution)/shard_map/all_to_all | solution.py:109
  (300 shorter events, 207.7 us)
Async XLA Ops:
  27.0 5.9 %copy-start.2 = (s32[64]{0:T(128)S(1)}, s32[64]{0:T(128)}, u32[]{:S(2)}) copy-start(s32[64]{0:T(128)} %param.11) | copy-start | bytes 772
  27.0 27.7 %all-to-all-start = ((bf16[8,2,49152]{2,1,0:T(2,128)(2,1)}), bf16[8,2,49152]{2,1,0:T(2,128)(2,1)S(1)}, u32[]{:S(2)}, u32[]{:S(2)}) async-start(bf16[8,2,49152]{2,1,0:T(2,128)(2,1)} %reshape.117), calls=%async_computation | async-start | bytes 3145728 | tf_op jit(solution)/shard_map/all_to_all | solution.py:89
  32.8 190.3 %all-gather.3.cloned.1.call-start = ((), (), s32[]{:S(2)}) async-start(), calls=%async_computation.2 | async-start | bytes 17301504 | tf_op jit(solution)/shard_map/all_gather | solution.py:74
  72.8 2.2 collective-permute-start
  78.9 1.4 copy-start
  78.9 1.4 copy-start.1
Sparse Core Ops, SparseCore 0:
  80.4 142.6 all-gather.2
where the time goes:
time: 534 us; the launch traced here: 531 us
  matrix products  175 us (33%)
  waiting for transfers between devices  163 us (31%)
  local copies, waits for them, and re-layouts  103 us (19%)
  other arithmetic  52.4 us (10%)
  blocking collectives  14.8 us (3%)
  between operations  13.6 us (3%)
  starting transfers between devices  7.36 us (1%)
    all_gather x1, waiting for transfers between devices, long_filter(): piece_rows = lax.all_gather(product, 'ctx', axis=0, tiled=True)  143 us
    dot_general x32, matrix products, filter_tile(): jnp.einsum('ejz,ejx->ezx', left_neighbor, right_neighbor, precision=lax.P...  119 us
    dynamic_slice x96, local copies, waits for them, and re-layouts, long_filter(): result, unused = lax.scan(scan_step, initial, (stacked, starts))  59.9 us
    dot_general x32, matrix products, split_product(): jnp.einsum(form, lower_part, inputs, preferred_element_type=jnp.float32)  31.6 us
    unnamed x13, local copies, waits for them, and re-layouts  28.1 us
    dot_general x32, matrix products, split_product(): jnp.einsum(form, upper_part, inputs, preferred_element_type=jnp.float32)  23.8 us
    sub x32, other arithmetic, filter_tile(): span - in_offsets  20.9 us
    sub x32, other arithmetic, filter_tile(): out_index - piece_start  20.7 us
  transfers between devices with their start and end apart: 3, of which 3 were waited for; matrix products, arithmetic and copies ran while one was open for 0% of the time, Pallas kernels for 0%

commit v1 on v0

--- a/solution.py
+++ b/solution.py
@@ -71,7 +71,9 @@
         return running + split_product("grs,sgc->rgc", token_tile_rows, inputs)
 
     initial = jnp.zeros((block_len, group_count, group_width), jnp.float32)
-    piece_rows = lax.all_gather(product, "ctx", axis=0, tiled=True)
+    piece_rows = jnp.concatenate(
+        lax.all_to_all(jnp.stack([product] * lax.axis_size("ctx")), "ctx", 0, 0), axis=0
+    )
     width_in = piece_rows.shape[0]
     count_blocks = width_in // block_len
     stacked = piece_rows.reshape(count_blocks, block_len, channels)

time: 534 us -> 845 us (1.58); the launches traced: 531 us -> 833 us
  waiting for transfers between devices: 163 us -> 379 us
  matrix products: 175 us -> 243 us
  starting transfers between devices: 7.36 us -> 23.3 us
  local copies, waits for them, and re-layouts: 103 us -> 117 us
  between operations: 13.6 us -> 0.18 us
    all_to_all x0 -> x1, waiting for transfers between devices: none -> 358 us  [long_filter(): lax.all_to_all(jnp.stack([product] * lax.axis_size('ctx')), 'ctx', 0, 0)]
    all_gather x1 -> x0, waiting for transfers between devices: 143 us -> none  [long_filter(): piece_rows = lax.all_gather(product, 'ctx', axis=0, tiled=True)]
    dot_general x32, matrix products: 31.6 us -> 100 us  [split_product(): jnp.einsum(form, lower_part, inputs, preferred_element_type=jnp.float32)]
    all_to_all x0 -> x1, starting transfers between devices: none -> 16.2 us  [long_filter(): lax.all_to_all(jnp.stack([product] * lax.axis_size('ctx')), 'ctx', 0, 0)]
    dynamic_slice x96 -> x64, local copies, waits for them, and re-layouts: 59.9 us -> 67.7 us  [long_filter(): result, unused = lax.scan(scan_step, initial, (stacked, starts))]
where the time goes in v1:
time: 845 us; the launch traced here: 833 us
  waiting for transfers between devices  379 us (45%)
  matrix products  243 us (29%)
  local copies, waits for them, and re-layouts  117 us (14%)
  other arithmetic  54.1 us (6%)
  starting transfers between devices  23.3 us (3%)
  blocking collectives  14 us (2%)
    all_to_all x1, waiting for transfers between devices, long_filter(): lax.all_to_all(jnp.stack([product] * lax.axis_size('ctx')), 'ctx', 0, 0)  358 us
    dot_general x32, matrix products, filter_tile(): jnp.einsum('ejz,ejx->ezx', left_neighbor, right_neighbor, precision=lax.P...  119 us
    dot_general x32, matrix products, split_product(): jnp.einsum(form, lower_part, inputs, preferred_element_type=jnp.float32)  100 us
    dynamic_slice x64, local copies, waits for them, and re-layouts, long_filter(): result, unused = lax.scan(scan_step, initial, (stacked, starts))  67.7 us
    unnamed x13, local copies, waits for them, and re-layouts  28.1 us
    dot_general x32, matrix products, split_product(): jnp.einsum(form, upper_part, inputs, preferred_element_type=jnp.float32)  24.1 us
    sub x32, other arithmetic, filter_tile(): span - in_offsets  21.8 us
    sub x32, other arithmetic, filter_tile(): out_index - piece_start  21.7 us
  transfers between devices with their start and end apart: 3, of which 3 were waited for; matrix products, arithmetic and copies ran while one was open for 0% of the time, Pallas kernels for 0%

profile of v1, /device:TPU:8, one launch (start us, length us, event | category | flops | bytes accessed | tf_op | source)
XLA Modules:
  0.0 833.3 jit_solution(14120530805532378818)
XLA Ops:
  0.0 10.6 %copy.24 = bf16[32,3,8192]{0,1,2:T(4,128)(2,1)} copy(bf16[32,3,8192]{2,0,1:T(8,128)(2,1)} %param.7) | data formatting | bytes 3145728 | tf_op args[0]
  10.6 9.8 %reshape.116 = bf16[8,2,49152]{2,1,0:T(2,128)(2,1)} reshape(bf16[8192,3,32]{2,1,0:T(4,128)(2,1)} %bitcast.55) | data formatting | bytes 3145728
  20.4 5.9 all-to-all-start
  28.5 19.6 %all-to-all-done = bf16[8,2,49152]{2,1,0:T(2,128)(2,1)S(1)} async-done(((bf16[8,2,49152]{2,1,0:T(2,128)(2,1)}), bf16[8,2,49152]{2,1,0:T(2,128)(2,1)S(1)}, u32[]{:S(2)}, u32[]{:S(2)}) %all-to-all-start) | async-done | bytes 1572896 | tf_op jit(solution)/shard_map/all_to_all | solution.py:91
  48.1 7.6 reshape.117
  55.7 10.5 %copy.32 = bf16[32,3,8,1024]{3,0,2,1:T(8,128)(2,1)S(1)} copy(bf16[32,3,8,1024]{0,1,3,2:T(4,128)(2,1)} %bitcast.54) | data formatting | bytes 3145728 | tf_op jit(solution)/shard_map/all_to_all | solution.py:91
  68.4 3.9 multiply_add_fusion
  73.8 5.9 stack.2
  79.7 16.2 %all-to-all-start.1 = ((bf16[32,256,1024]{1,2,0:T(8,128)(2,1)}), bf16[32,256,1024]{1,2,0:T(8,128)(2,1)}, u32[]{:S(2)}, u32[]{:S(2)}) async-start(bf16[32,256,1024]{1,2,0:T(8,128)(2,1)} %stack.2), calls=%async_computation.1 | async-start | bytes 33554432 | tf_op jit(solution)/shard_map/all_to_all | solution.py:75
  96.0 358.3 %all-to-all-done.1 = bf16[32,256,1024]{1,2,0:T(8,128)(2,1)} async-done(((bf16[32,256,1024]{1,2,0:T(8,128)(2,1)}), bf16[32,256,1024]{1,2,0:T(8,128)(2,1)}, u32[]{:S(2)}, u32[]{:S(2)}) %all-to-all-start.1) | async-done | bytes 16777248 | tf_op jit(solution)/shard_map/all_to_all | solution.py:75
  454.2 360.9 %while.13 = (s32[]{:T(128)}, f32[256,16,64]{0,2,1:T(8,128)S(1)}, bf16[32,256,1024]{1,2,0:T(8,128)(2,1)}, s32[32]{0:T(128)S(1)}, f32[16,16]{1,0:T(8,128)S(1)}, /*...) while((s32[]{:T(128)}, f32[256,16,64]{0,2,1:T(8,128)S(1)}, ...), condition=%wide.region_3.4_spmd.clone, body=%wide.region_2.3_spmd.clone.sunk | while | flops 477169920 | bytes 35856544 | solution.py:85
  455.6 3.7 fusion.43
  466.9 3.7 fusion.43
  478.1 3.7 fusion.43
  489.4 3.7 fusion.43
  500.7 3.7 fusion.43
  512.0 3.7 fusion.43
  523.2 3.7 fusion.43
  534.5 3.7 fusion.43
  557.1 3.7 fusion.43
  579.6 3.7 fusion.43
  602.2 3.7 fusion.43
  624.8 3.7 fusion.43
  647.3 3.7 fusion.43
  669.9 3.7 fusion.43
  692.4 3.7 fusion.43
  715.0 3.7 fusion.43
  737.6 3.7 fusion.43
  760.1 3.7 fusion.43
  782.7 3.7 fusion.43
  805.2 3.7 fusion.43
  818.5 14.0 %all_to_all.39 = bf16[8,32,1024]{2,1,0:T(8,128)(2,1)S(1)} all-to-all(bf16[8,32,1024]{2,1,0:T(8,128)(2,1)S(1)} %multiply_convert_fusion), channel_id=1, replica_groups=mesh['ctx'=32,'mp'=8] {'mp'}, dimensions={0} | all-to-all | bytes 1048576 | tf_op jit(solution)/shard_map/all_to_all | solution.py:111
  (333 shorter events, 293.6 us)
Async XLA Ops:
  20.4 5.9 copy-start.3
  20.4 27.7 %all-to-all-start = ((bf16[8,2,49152]{2,1,0:T(2,128)(2,1)}), bf16[8,2,49152]{2,1,0:T(2,128)(2,1)S(1)}, u32[]{:S(2)}, u32[]{:S(2)}) async-start(bf16[8,2,49152]{2,1,0:T(2,128)(2,1)} %reshape.116), calls=%async_computation | async-start | bytes 3145728 | tf_op jit(solution)/shard_map/all_to_all | solution.py:91
  66.3 2.2 collective-permute-start
  79.7 16.2 %copy-start.1 = (f32[16,16]{1,0:T(8,128)S(1)}, f32[16,16]{1,0:T(8,128)}, u32[]{:S(2)}) copy-start(f32[16,16]{1,0:T(8,128)} %param.10) | copy-start | bytes 3076
  79.7 16.2 %copy-start.2 = (f32[16,16]{1,0:T(8,128)S(1)}, f32[16,16]{1,0:T(8,128)}, u32[]{:S(2)}) copy-start(f32[16,16]{1,0:T(8,128)} %param.9) | copy-start | bytes 3076
  79.7 374.5 %all-to-all-start.1 = ((bf16[32,256,1024]{1,2,0:T(8,128)(2,1)}), bf16[32,256,1024]{1,2,0:T(8,128)(2,1)}, u32[]{:S(2)}, u32[]{:S(2)}) async-start(bf16[32,256,1024]{1,2,0:T(8,128)(2,1)} %stack.2), calls=%async_computation.1 | async-start | bytes 33554432 | tf_op jit(solution)/shard_map/all_to_all | solution.py:75
  459.3 2.3 copy-start
  470.6 2.3 copy-start
  481.9 2.3 copy-start
  493.1 2.3 copy-start
  504.4 2.3 copy-start
  515.7 2.3 copy-start
  527.0 2.3 copy-start
  538.3 2.3 copy-start
  549.5 2.3 copy-start
  560.8 2.3 copy-start
  572.1 2.3 copy-start
  583.4 2.3 copy-start
  594.7 2.3 copy-start
  605.9 2.3 copy-start
  617.2 2.3 copy-start
  628.5 2.3 copy-start
  639.8 2.3 copy-start
  651.1 2.3 copy-start
  662.3 2.3 copy-start
  673.6 2.3 copy-start
  696.2 2.3 copy-start
  718.7 2.3 copy-start
  741.3 2.3 copy-start
  763.9 2.3 copy-start
  786.4 2.3 copy-start
  809.0 2.3 copy-start
  (6 other events, 13.7 us)

commit v2 on v0

--- a/solution.py
+++ b/solution.py
@@ -86,7 +86,9 @@
 
 def shards(proj, conv_weight, residues, decays, doc_lengths):
     kernel_len = conv_weight.shape[1]
-    channel_rows = lax.all_to_all(proj, "mp", split_axis=2, concat_axis=0, tiled=True)
+    channel_rows = jnp.concatenate(
+        lax.all_to_all(jnp.stack(jnp.split(proj, lax.axis_size("mp"), axis=2)), "mp", 0, 0), axis=0
+    )
     block_len = channel_rows.shape[0]
     channels = channel_rows.shape[2]
     local_weight = lax.dynamic_slice_in_dim(

time: 534 us -> 508 us (0.951)
  local copies, waits for them, and re-layouts: 103 us -> 77.5 us
    unnamed x13 -> x17, local copies, waits for them, and re-layouts: 28.1 us -> 11.4 us
    all_to_all x1, local copies, waits for them, and re-layouts: 10.5 us -> 0.18 us  [shards(): lax.all_to_all(jnp.stack(jnp.split(proj, lax.axis_size('mp'), axis=2)), '...]
where the time goes in v2:
time: 508 us; the launch traced here: 506 us
  matrix products  175 us (34%)
  waiting for transfers between devices  163 us (32%)
  local copies, waits for them, and re-layouts  77.5 us (15%)
  other arithmetic  52.4 us (10%)
  blocking collectives  14.8 us (3%)
  between operations  13.6 us (3%)
  starting transfers between devices  7.05 us (1%)
    all_gather x1, waiting for transfers between devices, long_filter(): piece_rows = lax.all_gather(product, 'ctx', axis=0, tiled=True)  143 us
    dot_general x32, matrix products, filter_tile(): jnp.einsum('ejz,ejx->ezx', left_neighbor, right_neighbor, precision=lax.P...  119 us
    dynamic_slice x96, local copies, waits for them, and re-layouts, long_filter(): result, unused = lax.scan(scan_step, initial, (stacked, starts))  59.9 us
    dot_general x32, matrix products, split_product(): jnp.einsum(form, lower_part, inputs, preferred_element_type=jnp.float32)  31.6 us
    dot_general x32, matrix products, split_product(): jnp.einsum(form, upper_part, inputs, preferred_element_type=jnp.float32)  23.8 us
    sub x32, other arithmetic, filter_tile(): span - in_offsets  20.9 us
    sub x32, other arithmetic, filter_tile(): out_index - piece_start  20.7 us
    all_to_all x1, waiting for transfers between devices, shards(): lax.all_to_all(jnp.stack(jnp.split(proj, lax.axis_size('mp'), axis=2)), '...  19.6 us
  transfers between devices with their start and end apart: 3, of which 3 were waited for; matrix products, arithmetic and copies ran while one was open for 0% of the time, Pallas kernels for 0%

profile of v2, /device:TPU:8, one launch (start us, length us, event | category | flops | bytes accessed | tf_op | source)
XLA Modules:
  0.0 505.6 jit_solution(2499123381653605150)
XLA Ops:
  19.5 5.8 %all-to-all-start = ((bf16[8,32,3,1024]{3,1,2,0:T(8,128)(2,1)}), bf16[8,32,3,1024]{3,1,2,0:T(8,128)(2,1)S(1)}, u32[]{:S(2)}, u32[]{:S(2)}) async-start(bf16[8,32,3,1024]{3,1,2,0:T(8,128)(2,1)} %bitcast_dynamic-update-slice_fusion), calls=%async_computation | async-start | bytes 3145728 | tf_op jit(solution)/shard_map/all_to_all | solution.py:90
  27.4 19.6 %all-to-all-done = bf16[8,32,3,1024]{3,1,2,0:T(8,128)(2,1)S(1)} async-done(((bf16[8,32,3,1024]{3,1,2,0:T(8,128)(2,1)}), bf16[8,32,3,1024]{3,1,2,0:T(8,128)(2,1)S(1)}, u32[]{:S(2)}, u32[]{:S(2)}) %all-to-all-start) | async-done | bytes 1572896 | tf_op jit(solution)/shard_map/all_to_all | solution.py:90
  49.4 3.9 multiply_add_fusion
  54.8 142.8 %all-gather.3.cloned.1.call-done = bf16[8192,1,1024]{2,0,1:T(8,128)(2,1)} async-done(((bf16[256,1,1024]{2,0,1:T(8,128)(2,1)}), bf16[8192,1,1024]{2,0,1:T(8,128)(2,1)}) %all-gather.3.cloned.1.call-update) | async-done | bytes 16777232 | tf_op jit(solution)/shard_map/all_gather | solution.py:74
  197.6 282.1 %while.13 = (s32[]{:T(128)}, f32[256,16,64]{0,2,1:T(8,128)S(1)}, bf16[32,256,1024]{2,1,0:T(8,128)(2,1)}, s32[32]{0:T(128)S(1)}, f32[16,16]{1,0:T(8,128)S(1)}, /*...) while((s32[]{:T(128)}, f32[256,16,64]{0,2,1:T(8,128)S(1)}, ...), condition=%wide.region_3.4_spmd.clone, body=%wide.region_2.3_spmd.clone.sunk | while | flops 477169920 | bytes 20127888 | solution.py:83
  200.9 3.7 fusion.42
  209.7 3.7 fusion.42
  218.5 3.7 fusion.42
  227.3 3.7 fusion.42
  236.2 3.7 fusion.42
  245.0 3.7 fusion.42
  253.8 3.7 fusion.42
  262.6 3.7 fusion.42
  271.4 3.7 fusion.42
  280.2 3.7 fusion.42
  289.1 3.7 fusion.42
  297.9 3.7 fusion.42
  306.7 3.7 fusion.42
  315.5 3.7 fusion.42
  333.1 3.7 fusion.42
  342.0 3.7 fusion.42
  350.8 3.7 fusion.42
  359.6 3.7 fusion.42
  368.4 3.7 fusion.42
  377.2 3.7 fusion.42
  421.3 3.7 fusion.42
  430.1 3.7 fusion.42
  438.9 3.7 fusion.42
  447.8 3.7 fusion.42
  456.6 3.7 fusion.42
  465.4 3.7 fusion.42
  483.0 14.8 %all_to_all.21 = bf16[8,32,1024]{2,1,0:T(8,128)(2,1)S(1)} all-to-all(bf16[8,32,1024]{2,1,0:T(8,128)(2,1)S(1)} %multiply_convert_fusion), channel_id=1, replica_groups=mesh['ctx'=32,'mp'=8] {'mp'}, dimensions={0} | all-to-all | bytes 1048576 | tf_op jit(solution)/shard_map/all_to_all | solution.py:111
  (305 shorter events, 205.9 us)
Async XLA Ops:
  6.5 18.7 %copy-start.2 = (s32[64]{0:T(128)S(1)}, s32[64]{0:T(128)}, u32[]{:S(2)}) copy-start(s32[64]{0:T(128)} %param.11) | copy-start | bytes 772
  19.5 27.6 %all-to-all-start = ((bf16[8,32,3,1024]{3,1,2,0:T(8,128)(2,1)}), bf16[8,32,3,1024]{3,1,2,0:T(8,128)(2,1)S(1)}, u32[]{:S(2)}, u32[]{:S(2)}) async-start(bf16[8,32,3,1024]{3,1,2,0:T(8,128)(2,1)} %bitcast_dynamic-update-slice_fusion), calls=%async_computation | async-start | bytes 3145728 | tf_op jit(solution)/shard_map/all_to_all | solution.py:90
  25.2 172.4 %all-gather.3.cloned.1.call-start = ((), (), s32[]{:S(2)}) async-start(), calls=%async_computation.2 | async-start | bytes 17301504 | tf_op jit(solution)/shard_map/all_gather | solution.py:74
  47.3 2.2 collective-permute-start
  53.3 1.4 copy-start
  53.4 1.4 copy-start.1
Sparse Core Ops, SparseCore 0:
  54.9 142.6 all-gather.2
